TPU v7x, 32 devices: a whole 2x2x4 slice. The times are simulated.
32 devices in a mesh: groups: 1, wide: 32 (over z, y, x, core).
Axes of the slice: x: 2, y: 2, z: 4, core: 2. Of those that a mesh axis runs over, the one named last changes fastest.
Arguments:
- trial_bands: bfloat16 [1, 2, 3, 192, 192, 192], P('groups', None, None, 'wide'), may hold values from -160 to 160, as said below
- locked_bands: bfloat16 [4, 2, 3, 192, 192, 192], P('groups', None, None, 'wide'), may hold values from -240 to 240, as said below
- inv_diag: float32 [3, 192, 192, 192], P('groups', None, 'wide'), may hold values from 0.1 to 1
- inv_corr: float32 [3, 192, 192, 192], P('groups', None, 'wide'), may hold values from -0.3 to 0.3
Outputs:
- applied: bfloat16 [1, 2, 3, 192, 192, 192], P('groups', None, None, 'wide')
- rayleigh: float32 [2, 1, 1], P('groups')
Inputs may be any that keep to these rules, and one draw needn't show every extreme that they name: `trial_bands`: sums of locked and independent fields, bounded. `locked_bands`: the locked bands are linearly independent.
All inputs are finite; a program needn't handle non-finite values.
Results may differ from a plain program's by a relative error of at most 0.0013.
Values sent between devices are 32-bit elements; how exact they have to be, the bound alone decides.
No kernel may reach another device: no remote copies, remote signals or barrier semaphores. Data moves between devices by JAX's collectives and lax.ppermute only.
A program may use at most 128 MiB of HBM per device.

v0:
```python
import functools
import math

import ml_dtypes
import numpy as np

import jax
import jax.numpy as jnp
from jax import lax
from jax.sharding import PartitionSpec as P
from jax.experimental import pallas as pl
from jax.experimental.pallas import tpu as pltpu

highest = lax.Precision.HIGHEST
three_pass = lax.Precision.HIGH


def signed_wave(indices, length):
    shifted = jnp.where(indices < length // 2, indices, indices - length)
    return shifted.astype(jnp.float32) / (length / 2.0)


def cross_wave(wave_x, wave_y, wave_z, vectors):
    comp_x = vectors[..., 0, :, :, :]
    comp_y = vectors[..., 1, :, :, :]
    comp_z = vectors[..., 2, :, :, :]
    along_x = wave_x[:, None, None]
    along_y = wave_y[None, :, None]
    along_z = wave_z[None, None, :]
    return jnp.stack(
        [
            along_y * comp_z - along_z * comp_y,
            along_z * comp_x - along_x * comp_z,
            along_x * comp_y - along_y * comp_x,
        ],
        axis=-4,
    )


def curl_times_i(waves, stacked):
    wave_x, wave_y, wave_z = waves
    return jnp.stack(
        [
            -cross_wave(wave_x, wave_y, wave_z, stacked[1]),
            cross_wave(wave_x, wave_y, wave_z, stacked[0]),
        ],
        axis=0,
    )


def apply_tensor(vectors, inv_diag, inv_corr):
    coupling_xy = inv_corr[0] * jnp.sqrt(inv_diag[0] * inv_diag[1])
    coupling_xz = inv_corr[1] * jnp.sqrt(inv_diag[0] * inv_diag[2])
    coupling_yz = inv_corr[2] * jnp.sqrt(inv_diag[1] * inv_diag[2])
    comp_x = vectors[..., 0, :, :, :]
    comp_y = vectors[..., 1, :, :, :]
    comp_z = vectors[..., 2, :, :, :]
    out_x = inv_diag[0] * comp_x + coupling_xy * comp_y + coupling_xz * comp_z
    out_y = coupling_xy * comp_x + inv_diag[1] * comp_y + coupling_yz * comp_z
    out_z = coupling_xz * comp_x + coupling_yz * comp_y + inv_diag[2] * comp_z
    return jnp.stack([out_x, out_y, out_z], axis=-4)


def complex_table(length, orient):
    indices = jnp.arange(length, dtype=jnp.int32)
    phases = indices[:, None] * indices[None, :] % length
    angles = phases.astype(jnp.float32) * (2.0 * math.pi / length)
    norm_factor = 1.0 / math.sqrt(length)
    cos_table = jnp.cos(angles) * norm_factor
    sin_table = jnp.sin(angles) * norm_factor * orient
    return jnp.stack(
        [jnp.stack([cos_table, sin_table], axis=0), jnp.stack([-sin_table, cos_table], axis=0)],
        axis=0,
    )


def transform(stacked, axis_dim, orient):
    table = complex_table(stacked.shape[axis_dim + 1], orient)
    if axis_dim == 2:
        return jnp.einsum("pbckyz,pqkn->qbcnyz", stacked, table, precision=three_pass)
    if axis_dim == 3:
        return jnp.einsum("pbcxkz,pqkn->qbcxnz", stacked, table, precision=three_pass)
    return jnp.einsum("pbcxyk,pqkn->qbcxyn", stacked, table, precision=three_pass)


def split_hi_lo(values):
    scaled = values * 65537.0
    top = scaled - (scaled - values)
    return top.astype(jnp.bfloat16), (values - top).astype(jnp.bfloat16)


def dot_right(values, table_hi, table_lo):
    high, low = split_hi_lo(values)
    f32 = jnp.float32
    return (
        jnp.dot(high, table_hi, preferred_element_type=f32)
        + jnp.dot(low, table_hi, preferred_element_type=f32)
        + jnp.dot(high, table_lo, preferred_element_type=f32)
    )


def dot_left(table_hi, table_lo, values):
    high, low = split_hi_lo(values)
    f32 = jnp.float32
    return (
        jnp.dot(table_hi, high, preferred_element_type=f32)
        + jnp.dot(table_hi, low, preferred_element_type=f32)
        + jnp.dot(table_lo, high, preferred_element_type=f32)
    )


def front_kernel(comps, coef_ref, qx_ref, trial_ref, locked_ref, chi_ref, clo_ref, shi_ref, slo_ref, out_ref):
    band = pl.program_id(0)
    plane = pl.program_id(1)
    kept = locked_ref.shape[0]
    size = trial_ref.shape[-1]
    f32 = jnp.float32
    first = [coef_ref[band, k] for k in range(kept)]
    second = [coef_ref[band, kept + k] for k in range(kept)]
    needed = sorted({(c + 1) % 3 for c in comps} | {(c + 2) % 3 for c in comps})
    part_re = {}
    part_im = {}
    for comp in needed:
        acc_re = trial_ref[0, 0, comp, 0].astype(f32)
        acc_im = trial_ref[0, 1, comp, 0].astype(f32)
        for k in range(kept):
            l_re = locked_ref[k, 0, comp, 0].astype(f32)
            l_im = locked_ref[k, 1, comp, 0].astype(f32)
            acc_re = acc_re - first[k] * l_re + second[k] * l_im
            acc_im = acc_im - first[k] * l_im - second[k] * l_re
        part_re[comp] = acc_re
        part_im[comp] = acc_im
    rows = lax.broadcasted_iota(jnp.int32, (size, 1), 0)
    cols = lax.broadcasted_iota(jnp.int32, (1, size), 1)
    half = size // 2
    wave_y = jnp.where(rows < half, rows, rows - size).astype(f32) / (size / 2.0)
    wave_z = jnp.where(cols < half, cols, cols - size).astype(f32) / (size / 2.0)
    waves = (qx_ref[plane], wave_y, wave_z)
    c_hi = chi_ref[...]
    c_lo = clo_ref[...]
    s_hi = shi_ref[...]
    s_lo = slo_ref[...]
    for slot, comp in enumerate(comps):
        a = (comp + 1) % 3
        b = (comp + 2) % 3
        cur_re = -(waves[a] * part_im[b] - waves[b] * part_im[a])
        cur_im = waves[a] * part_re[b] - waves[b] * part_re[a]
        z_re = dot_right(cur_re, c_hi, c_lo) - dot_right(cur_im, s_hi, s_lo)
        z_im = dot_right(cur_re, s_hi, s_lo) + dot_right(cur_im, c_hi, c_lo)
        y_re = dot_left(c_hi, c_lo, z_re) - dot_left(s_hi, s_lo, z_im)
        y_im = dot_left(s_hi, s_lo, z_re) + dot_left(c_hi, c_lo, z_im)
        out_ref[0, 0, slot, 0] = y_re
        out_ref[1, 0, slot, 0] = y_im


def numpy_split(table):
    full = table.astype(np.float32)
    high = full.astype(ml_dtypes.bfloat16)
    low = (full - high.astype(np.float32)).astype(ml_dtypes.bfloat16)
    return jnp.asarray(high), jnp.asarray(low)


def dft_tables(length, orient):
    indices = np.arange(length, dtype=np.int64)
    phases = indices[:, None] * indices[None, :] % length
    angles = phases.astype(np.float64) * (2.0 * math.pi / length)
    norm_factor = 1.0 / math.sqrt(length)
    c_hi, c_lo = numpy_split(np.cos(angles) * norm_factor)
    s_hi, s_lo = numpy_split(np.sin(angles) * norm_factor * orient)
    return c_hi, c_lo, s_hi, s_lo


def front_pass(comps, coef_rows, wave_x, trial_bands, locked_bands):
    band_count, _, _, local_x, size, _ = trial_bands.shape
    kept = locked_bands.shape[0]
    tables = dft_tables(size, 1.0)
    smem = pl.BlockSpec(memory_space=pltpu.SMEM)
    table_spec = pl.BlockSpec((size, size), lambda b, x: (0, 0))
    width = len(comps)
    return pl.pallas_call(
        functools.partial(front_kernel, comps),
        grid=(band_count, local_x),
        in_specs=[
            smem,
            smem,
            pl.BlockSpec((1, 2, 3, 1, size, size), lambda b, x: (b, 0, 0, x, 0, 0)),
            pl.BlockSpec((kept, 2, 3, 1, size, size), lambda b, x: (0, 0, 0, x, 0, 0)),
            table_spec,
            table_spec,
            table_spec,
            table_spec,
        ],
        out_specs=pl.BlockSpec((2, 1, width, 1, size, size), lambda b, x: (0, b, 0, x, 0, 0)),
        out_shape=jax.ShapeDtypeStruct((2, band_count, width, local_x, size, size), jnp.float32),
    )(coef_rows, wave_x, trial_bands, locked_bands, *tables)


def radix_sum(values, axis, count):
    if count & (count - 1):
        return lax.psum(values, axis)
    me = lax.axis_index(axis)
    stride = 1
    while stride < count:
        radix = 4 if count // stride >= 4 else 2
        digit = (me // stride) % radix
        slots = [None] * radix
        for offset in range(radix):
            if offset == 0:
                got = values
            else:
                pairs = []
                for dst in range(count):
                    dst_digit = (dst // stride) % radix
                    base = dst - dst_digit * stride
                    pairs.append((base + ((dst_digit + offset) % radix) * stride, dst))
                got = lax.ppermute(values, axis, pairs)
            slots[offset] = got
        ordered = []
        for member in range(radix):
            pick = slots[0]
            for offset in range(1, radix):
                pick = jnp.where((digit + offset) % radix == member, slots[offset], pick)
            ordered.append(pick)
        total = ordered[0]
        for member in range(1, radix):
            total = total + ordered[member]
        values = total
        stride *= radix
    return values


def butterfly_sum(values, axis, count):
    if count & (count - 1):
        return lax.psum(values, axis)
    step = 1
    while step < count:
        pairs = [(index, index ^ step) for index in range(count)]
        values = values + lax.ppermute(values, axis, pairs)
        step *= 2
    return values


def inner_sum(left_rows, right_rows):
    return jnp.einsum("an,bn->ab", left_rows, right_rows, preferred_element_type=jnp.float32)


def remove_locked(gram_sums, trial_re, trial_im, locked_re, locked_im):
    gram_a, gram_q, proj_re, proj_im = gram_sums
    kept_count = gram_a.shape[0]
    gram = jnp.concatenate(
        [jnp.concatenate([gram_a, gram_q], axis=1), jnp.concatenate([gram_q.T, gram_a], axis=1)],
        axis=0,
    )
    rhs_both = jnp.concatenate([proj_re, proj_im], axis=0)
    lower = jnp.linalg.cholesky(gram)
    middle = lax.linalg.triangular_solve(lower, rhs_both, left_side=True, lower=True)
    coef = lax.linalg.triangular_solve(lower, middle, left_side=True, lower=True, transpose_a=True)
    coef_one = coef[:kept_count]
    coef_two = coef[kept_count:]
    locked_re32 = locked_re.astype(jnp.float32)
    locked_im32 = locked_im.astype(jnp.float32)
    out_re = (
        trial_re.astype(jnp.float32)
        - jnp.einsum("ab,an->bn", coef_one, locked_re32, precision=highest)
        + jnp.einsum("ab,an->bn", coef_two, locked_im32, precision=highest)
    )
    out_im = (
        trial_im.astype(jnp.float32)
        - jnp.einsum("ab,an->bn", coef_one, locked_im32, precision=highest)
        - jnp.einsum("ab,an->bn", coef_two, locked_re32, precision=highest)
    )
    return (out_re, out_im)


def solve_coef(gram_sums):
    gram_a, gram_q, proj_re, proj_im = gram_sums
    gram = jnp.concatenate(
        [jnp.concatenate([gram_a, gram_q], axis=1), jnp.concatenate([gram_q.T, gram_a], axis=1)],
        axis=0,
    )
    rhs_both = jnp.concatenate([proj_re, proj_im], axis=0)
    lower = jnp.linalg.cholesky(gram)
    middle = lax.linalg.triangular_solve(lower, rhs_both, left_side=True, lower=True)
    return lax.linalg.triangular_solve(lower, middle, left_side=True, lower=True, transpose_a=True)


def maxwell_pass(chunks, waves, inv_diag, inv_corr, to_space_fn, to_spectrum_fn):
    space = jnp.concatenate([transform(to_space_fn(chunk), 2, 1.0) for chunk in chunks], axis=2)
    weighted = apply_tensor(space, inv_diag, inv_corr)
    homes = []
    for comp in range(weighted.shape[2]):
        source = transform(weighted[:, :, comp : comp + 1], 2, -1.0)
        if comp >= 2:
            source, _ = lax.optimization_barrier((source, homes[comp - 2]))
        home = to_spectrum_fn(source)
        home = transform(home, 3, -1.0)
        homes.append(transform(home, 4, -1.0))
    home = jnp.concatenate(homes, axis=2)
    return (curl_times_i(waves, home), space, weighted)


def per_device(wide_count, trial_bands, locked_bands, inv_diag, inv_corr):
    band_count = trial_bands.shape[0]
    kept_count = locked_bands.shape[0]
    local_x = trial_bands.shape[3]
    grid_len = trial_bands.shape[4]
    rows = jnp.concatenate(
        [locked_bands.reshape((2 * kept_count,) + locked_bands.shape[2:]),
         trial_bands.reshape((2 * band_count,) + trial_bands.shape[2:])],
        axis=0,
    )
    pairs = jnp.einsum("icxyz,jcxyz->ij", rows, rows, preferred_element_type=jnp.float32)
    pairs = radix_sum(pairs, "wide", wide_count)
    lk = pairs[: 2 * kept_count, : 2 * kept_count].reshape(kept_count, 2, kept_count, 2)
    lt = pairs[: 2 * kept_count, 2 * kept_count :].reshape(kept_count, 2, band_count, 2)
    gram_a = lk[:, 0, :, 0] + lk[:, 1, :, 1]
    gram_q = lk[:, 1, :, 0] - lk[:, 0, :, 1]
    proj_re = lt[:, 0, :, 0] + lt[:, 1, :, 1]
    proj_im = lt[:, 0, :, 1] - lt[:, 1, :, 0]
    gram_sums = (gram_a, gram_q, proj_re, proj_im)
    coef = solve_coef(gram_sums)
    start_x = lax.axis_index("wide") * local_x
    full_axis = jnp.arange(grid_len, dtype=jnp.int32)
    wave_x = signed_wave(start_x + jnp.arange(local_x, dtype=jnp.int32), grid_len)
    wave_full = signed_wave(full_axis, grid_len)
    waves = (wave_x, wave_full, wave_full)

    def exchange_rows(field, split_dim, keep_dim):
        parts, bands, comps = field.shape[0], field.shape[1], field.shape[2]
        order = (split_dim, 1, 2, keep_dim, 0, 5)
        moved = jnp.transpose(field, order).reshape(wide_count, -1, 128)
        moved = lax.all_to_all(moved, "wide", split_axis=0, concat_axis=0, tiled=True)
        local_split = field.shape[split_dim] // wide_count
        moved = moved.reshape(
            wide_count, local_split, bands, comps, field.shape[keep_dim], parts, field.shape[5]
        )
        return moved

    def send_out_one(field):
        moved = exchange_rows(field, 4, 3)
        moved = jnp.transpose(moved, (5, 2, 3, 0, 4, 1, 6))
        shape = moved.shape
        return moved.reshape(shape[0], shape[1], shape[2], shape[3] * shape[4], shape[5], shape[6])

    def send_home_one(field):
        moved = exchange_rows(field, 3, 4)
        moved = jnp.transpose(moved, (5, 2, 3, 1, 0, 4, 6))
        shape = moved.shape
        return moved.reshape(shape[0], shape[1], shape[2], shape[3], shape[4] * shape[5], shape[6])

    chunks = [front_pass((comp,), coef.T, wave_x, trial_bands, locked_bands) for comp in range(3)]
    results = [maxwell_pass(chunks, waves, inv_diag, inv_corr, send_out_one, send_home_one)]
    applied_st, space, weighted = [
        jnp.concatenate([entry[slot] for entry in results], axis=1) for slot in range(3)
    ]
    applied = jnp.stack([applied_st[0], applied_st[1]], axis=1).astype(jnp.bfloat16)
    scale_all = 1.0 / float(grid_len * grid_len * grid_len)
    left_re = space[0].reshape(band_count, -1)
    left_im = space[1].reshape(band_count, -1)
    right_re = weighted[0].reshape(band_count, -1)
    right_im = weighted[1].reshape(band_count, -1)
    part_re = jnp.einsum("an,bn->ab", left_re, right_re, precision=highest) + jnp.einsum(
        "an,bn->ab", left_im, right_im, precision=highest
    )
    part_im = jnp.einsum("an,bn->ab", left_re, right_im, precision=highest) - jnp.einsum(
        "an,bn->ab", left_im, right_re, precision=highest
    )
    total_re, total_im = butterfly_sum(jnp.stack([part_re, part_im], axis=0), "wide", wide_count)
    rayleigh = jnp.stack([total_re * scale_all, total_im * scale_all], axis=0)
    return (applied, rayleigh)


def solution(mesh):
    in_specs = (
        P("groups", None, None, "wide", None, None),
        P("groups", None, None, "wide", None, None),
        P("groups", None, "wide", None),
        P("groups", None, "wide", None),
    )
    out_specs = (P("groups", None, None, "wide", None, None), P("groups", None, None))
    wide_count = mesh.shape["wide"]
    return jax.shard_map(
        functools.partial(per_device, wide_count), mesh=mesh, in_specs=in_specs, out_specs=out_specs, check_vma=False
    )
```

profile of v0, /device:TPU:0, one launch (start us, length us, event | category | flops | bytes accessed | tf_op | source)
XLA Modules:
  0.0 417.6 jit_solution(5688159909407539346)
XLA Ops:
  0.6 5.7 %copy.235 = bf16[1,2,3,6,192,192]{5,1,4,3,2,0:T(2,128)(2,1)S(1)} copy(bf16[1,2,3,6,192,192]{5,4,3,2,1,0:T(8,128)(2,1)} %trial_ref.5) | data formatting | bytes 5308416 | tf_op args[0]
  6.3 13.6 %copy.133 = bf16[8,3,6,192,192]{4,0,3,2,1:T(8,128)(2,1)S(1)} copy(bf16[8,3,6,192,192]{4,3,2,1,0:T(8,128)(2,1)} %bitcast.339) | data formatting | bytes 21233664 | tf_op jit(solution)/shard_map/reshape | solution.py:308
  19.9 16.5 %fusion.75 = f32[10,10]{0,1:T(8,128)S(1)} fusion(bf16[2,3,6,192,192]{4,0,3,2,1:T(2,128)(2,1)S(1)} %bitcast.362, bf16[8,3,6,192,192]{4,0,3,2,1:T(8,128)(2,1)S(1)} %copy.133), kind=kOutput, calls=%fused_computation.95 | convolution fusion | flops 159252480 | bytes 13271440 | tf_op jit(solution)/shard_map/icxyz,jcxyz->ij/dot_general | solution.py:312
  37.0 2.6 collective-permute-start.1
  49.3 2.7 collective-permute-start.6
  58.5 12.9 %shard_map.168 = f32[2,1,1,6,192,192]{5,4,3,2,1,0:T(8,128)} custom-call(f32[1,8]{1,0:T(1,128)} %fusion.104.coef_ref, f32[6]{0:T(128)} %fusion.112.qx_ref, bf16[1,2,3,6,192,192]{5,4,3,2,1,0:T(8,128)(2,1)} %trial_ref.5, bf16[4,2,3,6,192,192]{5,4,3,2,1,0:T(8,128)(2,1)} %locked_ref.5, bf16[192,192]{1,0:T(8,128)(2,1)} %constant.252.clone.chi_ref, ...), custom_call_target="tpu_custom_call" | custom-call | tf_op jit(solution)/shard_map/pallas_call | solution.py:180
  71.4 3.5 copy.56
  74.9 3.1 reshape.595
  78.0 5.1 %all-to-all-start.1 = ((f32[32,108,128]{2,1,0:T(8,128)}), f32[32,108,128]{2,1,0:T(8,128)}, u32[]{:S(2)}, u32[]{:S(2)}) async-start(f32[32,108,128]{2,1,0:T(8,128)} %reshape.595), calls=%async_computation.1 | async-start | bytes 3670016 | tf_op jit(solution)/shard_map/all_to_all | solution.py:332
  83.2 13.1 %shard_map.167 = f32[2,1,1,6,192,192]{5,4,3,2,1,0:T(8,128)} custom-call(f32[1,8]{1,0:T(1,128)} %fusion.104.coef_ref, f32[6]{0:T(128)} %fusion.112.qx_ref, bf16[1,2,3,6,192,192]{5,4,3,2,1,0:T(8,128)(2,1)} %trial_ref.5, bf16[4,2,3,6,192,192]{5,4,3,2,1,0:T(8,128)(2,1)} %locked_ref.5, bf16[192,192]{1,0:T(8,128)(2,1)} %constant.252.clone.chi_ref, ...), custom_call_target="tpu_custom_call" | custom-call | tf_op jit(solution)/shard_map/pallas_call | solution.py:180
  96.2 3.5 copy.53
  99.7 3.1 reshape.592
  102.9 23.5 %all-to-all-done.1 = f32[32,108,128]{2,1,0:T(8,128)} async-done(((f32[32,108,128]{2,1,0:T(8,128)}), f32[32,108,128]{2,1,0:T(8,128)}, u32[]{:S(2)}, u32[]{:S(2)}) %all-to-all-start.1) | async-done | bytes 1769504 | tf_op jit(solution)/shard_map/all_to_all | solution.py:332
  126.4 4.1 all-to-all-start
  130.5 13.1 %shard_map.169 = f32[2,1,1,6,192,192]{5,4,3,2,1,0:T(8,128)} custom-call(f32[1,8]{1,0:T(1,128)} %fusion.104.coef_ref, f32[6]{0:T(128)} %fusion.112.qx_ref, bf16[1,2,3,6,192,192]{5,4,3,2,1,0:T(8,128)(2,1)} %trial_ref.5, bf16[4,2,3,6,192,192]{5,4,3,2,1,0:T(8,128)(2,1)} %locked_ref.5, bf16[192,192]{1,0:T(8,128)(2,1)} %constant.252.clone.chi_ref, ...), custom_call_target="tpu_custom_call" | custom-call | tf_op jit(solution)/shard_map/pallas_call | solution.py:180
  143.6 3.5 copy.59
  147.1 3.1 reshape.598
  150.2 23.5 %all-to-all-done = f32[32,108,128]{2,1,0:T(8,128)} async-done(((f32[32,108,128]{2,1,0:T(8,128)}), f32[32,108,128]{2,1,0:T(8,128)}, u32[]{:S(2)}, u32[]{:S(2)}) %all-to-all-start) | async-done | bytes 1769504 | tf_op jit(solution)/shard_map/all_to_all | solution.py:332
  173.7 4.5 %all-to-all-start.2 = ((f32[32,108,128]{2,1,0:T(8,128)}), f32[32,108,128]{2,1,0:T(8,128)}, u32[]{:S(2)}, u32[]{:S(2)}) async-start(f32[32,108,128]{2,1,0:T(8,128)} %reshape.598), calls=%async_computation.2 | async-start | bytes 3670016 | tf_op jit(solution)/shard_map/all_to_all | solution.py:332
  187.3 2.9 reshape.596
  192.5 2.9 reshape.593
  199.4 3.6 fusion.33
  203.0 18.5 %all-to-all-done.2 = f32[32,108,128]{2,1,0:T(8,128)} async-done(((f32[32,108,128]{2,1,0:T(8,128)}), f32[32,108,128]{2,1,0:T(8,128)}, u32[]{:S(2)}, u32[]{:S(2)}) %all-to-all-start.2) | async-done | bytes 1769504 | tf_op jit(solution)/shard_map/all_to_all | solution.py:332
  221.5 4.1 reshape.599
  225.6 2.6 copy.60
  228.4 7.1 %fusion.24 = (f32[2,192,6,192]{3,1,2,0:T(8,128)}, f32[2,192,6,192]{3,1,2,0:T(8,128)}, f32[2,192,6,192]{3,1,2,0:T(8,128)S(1)}, f32[2,192,6,192,1]{3,1,4,2,0:T(8,128)}) fusion(f32[2,192,6,192,1]{3,1,4,2,0:T(8,128)S(1)} %fusion.31, f32[2,192,6,192,1]{3,1,4,2,0:T(8,128)S(1)} %copy-done, f32[192,6,192]{2,0,1:T(8,128)} %get-tuple-element.20, ...), kind=kOutput, calls=%fused_computation.43 | convolution fusion | flops 1025998848 | bytes 18284544 | tf_op jit(solution)/shard_map/pbckyz,pqkn->qbcnyz/dot_general | solution.py:80
  237.8 3.2 copy.64
  241.0 4.4 %reshape.601 = f32[32,108,128]{2,1,0:T(8,128)} reshape(f32[192,1,1,6,2,192]{5,4,3,0,2,1:T(2,128)} %copy.64) | data formatting | bytes 3538944 | tf_op jit(solution)/shard_map/reshape | solution.py:331
  245.4 4.1 all-to-all-start.3
  249.5 3.7 fusion.57
  253.3 3.2 copy.72
  256.5 4.4 %reshape.605 = f32[32,108,128]{2,1,0:T(8,128)} reshape(f32[192,1,1,6,2,192]{5,4,3,0,2,1:T(2,128)} %copy.72) | data formatting | bytes 3538944 | tf_op jit(solution)/shard_map/reshape | solution.py:331
  260.8 31.9 %all-to-all-done.3 = f32[32,108,128]{2,1,0:T(8,128)} async-done(((f32[32,108,128]{2,1,0:T(8,128)}), f32[32,108,128]{2,1,0:T(8,128)}, u32[]{:S(2)}, u32[]{:S(2)}) %all-to-all-start.3) | async-done | bytes 1769504 | tf_op jit(solution)/shard_map/all_to_all | solution.py:332
  292.7 4.4 %all-to-all-start.4 = ((f32[32,108,128]{2,1,0:T(8,128)}), f32[32,108,128]{2,1,0:T(8,128)}, u32[]{:S(2)}, u32[]{:S(2)}) async-start(f32[32,108,128]{2,1,0:T(8,128)} %reshape.605), calls=%async_computation.4 | async-start | bytes 3670016 | tf_op jit(solution)/shard_map/all_to_all | solution.py:332
  297.1 5.2 %fusion.66 = f32[2,1,1,192,6,192]{5,3,4,0,2,1:T(8,128)} fusion(f32[2,192,6,192]{3,1,2,0:T(8,128)} %get-tuple-element.15, f32[1,2,192,192]{2,3,1,0:T(8,128)S(1)} %get-tuple-element.34, f32[1,2,192,192]{2,3,1,0:T(8,128)S(1)} %get-tuple-element.31), kind=kOutput, calls=%fused_computation.80 | convolution fusion | flops 1019363328 | bytes 4128768 | tf_op jit(solution)/shard_map/pbckyz,pqkn->qbcnyz/dot_general | solution.py:80
  302.3 3.9 reshape.602
  310.9 3.5 fusion.54
  314.4 3.3 copy.80
  317.6 4.4 %reshape.609 = f32[32,108,128]{2,1,0:T(8,128)} reshape(f32[192,1,1,6,2,192]{5,4,3,0,2,1:T(2,128)} %copy.80) | data formatting | bytes 3538944 | tf_op jit(solution)/shard_map/reshape | solution.py:331
  322.0 18.3 %all-to-all-done.4 = f32[32,108,128]{2,1,0:T(8,128)} async-done(((f32[32,108,128]{2,1,0:T(8,128)}), f32[32,108,128]{2,1,0:T(8,128)}, u32[]{:S(2)}, u32[]{:S(2)}) %all-to-all-start.4) | async-done | bytes 1769504 | tf_op jit(solution)/shard_map/all_to_all | solution.py:332
  340.3 4.5 %all-to-all-start.5 = ((f32[32,108,128]{2,1,0:T(8,128)}), f32[32,108,128]{2,1,0:T(8,128)}, u32[]{:S(2)}, u32[]{:S(2)}) async-start(f32[32,108,128]{2,1,0:T(8,128)} %reshape.609), calls=%async_computation.5 | async-start | bytes 3670016 | tf_op jit(solution)/shard_map/all_to_all | solution.py:332
  344.9 3.0 pad_maximum_fusion.1
  365.0 10.7 %collective-permute-done.10 = f32[2,1,1]{0,2,1:T(1,128)S(1)} collective-permute-done((f32[2,1,1]{0,2,1:T(1,128)S(1)}, f32[2,1,1]{0,2,1:T(1,128)S(1)}, u32[]{:S(2)}, u32[]{:S(2)}) %collective-permute-start.10) | collective-permute-done | bytes 40 | tf_op jit(solution)/shard_map/ppermute | solution.py:238
  375.7 3.8 collective-permute-start.11
  379.5 8.5 %collective-permute-done.11 = f32[2,1,1]{0,2,1:T(1,128)S(1)} collective-permute-done((f32[2,1,1]{0,2,1:T(1,128)S(1)}, f32[2,1,1]{0,2,1:T(1,128)S(1)}, u32[]{:S(2)}, u32[]{:S(2)}) %collective-permute-start.11) | collective-permute-done | bytes 40 | tf_op jit(solution)/shard_map/ppermute | solution.py:238
  390.5 2.9 reshape.606
  398.6 4.1 reshape.610
  413.7 3.7 copy.87
  (106 shorter events, 70.7 us)
Async XLA Ops:
  36.5 5.0 %collective-permute-start = (f32[10,10]{0,1:T(8,128)S(1)}, f32[10,10]{0,1:T(8,128)S(1)}, u32[]{:S(2)}, u32[]{:S(2)}) collective-permute-start(f32[10,10]{0,1:T(8,128)S(1)} %fusion.75), channel_id=1, source_target_pairs={{3,0},{0,1},{1,2},{2,3},{7,4},{4,5},{5,6},{6,7},{11,8},{8,9},{9,10... | collective-permute-start | bytes 1208 | tf_op jit(solution)/shard_map/ppermute | solution.py:216
  37.0 4.5 %collective-permute-start.1 = (f32[10,10]{0,1:T(8,128)S(1)}, f32[10,10]{0,1:T(8,128)S(1)}, u32[]{:S(2)}, u32[]{:S(2)}) collective-permute-start(f32[10,10]{0,1:T(8,128)S(1)} %fusion.75), channel_id=1, source_target_pairs={{2,0},{3,1},{0,2},{1,3},{6,4},{7,5},{4,6},{5,7},{10,8},{11,9},{8,1... | collective-permute-start | bytes 1208 | tf_op jit(solution)/shard_map/ppermute | solution.py:216
  39.5 2.8 collective-permute-start.2
  42.3 4.7 %collective-permute-start.3 = (f32[10,10]{0,1:T(8,128)S(1)}, f32[10,10]{0,1:T(8,128)S(1)}, u32[]{:S(2)}, u32[]{:S(2)}) collective-permute-start(f32[10,10]{0,1:T(8,128)S(1)} %select_add_fusion.2), channel_id=1, source_target_pairs={{12,0},{13,1},{14,2},{15,3},{0,4},{1,5},{2,6},{3,7},{4,8},{5,9},{6... | collective-permute-start | bytes 1208 | tf_op jit(solution)/shard_map/ppermute | solution.py:216
  43.9 3.7 collective-permute-start.4
  45.4 3.8 collective-permute-start.5
  49.3 4.6 %collective-permute-start.6 = (f32[10,10]{0,1:T(8,128)S(1)}, f32[10,10]{0,1:T(8,128)S(1)}, u32[]{:S(2)}, u32[]{:S(2)}) collective-permute-start(f32[10,10]{0,1:T(8,128)S(1)} %select_add_fusion.1), channel_id=1, source_target_pairs={{16,0},{17,1},{18,2},{19,3},{20,4},{21,5},{22,6},{23,7},{24,8},{25... | collective-permute-start | bytes 1208 | tf_op jit(solution)/shard_map/ppermute | solution.py:216
  78.0 48.4 %all-to-all-start.1 = ((f32[32,108,128]{2,1,0:T(8,128)}), f32[32,108,128]{2,1,0:T(8,128)}, u32[]{:S(2)}, u32[]{:S(2)}) async-start(f32[32,108,128]{2,1,0:T(8,128)} %reshape.595), calls=%async_computation.1 | async-start | bytes 3670016 | tf_op jit(solution)/shard_map/all_to_all | solution.py:332
  126.4 47.4 %all-to-all-start = ((f32[32,108,128]{2,1,0:T(8,128)}), f32[32,108,128]{2,1,0:T(8,128)}, u32[]{:S(2)}, u32[]{:S(2)}) async-start(f32[32,108,128]{2,1,0:T(8,128)} %reshape.592), calls=%async_computation | async-start | bytes 3670016 | tf_op jit(solution)/shard_map/all_to_all | solution.py:332
  173.7 47.8 %all-to-all-start.2 = ((f32[32,108,128]{2,1,0:T(8,128)}), f32[32,108,128]{2,1,0:T(8,128)}, u32[]{:S(2)}, u32[]{:S(2)}) async-start(f32[32,108,128]{2,1,0:T(8,128)} %reshape.598), calls=%async_computation.2 | async-start | bytes 3670016 | tf_op jit(solution)/shard_map/all_to_all | solution.py:332
  178.3 3.3 copy-start.5
  181.6 3.3 copy-start.12
  195.4 1.7 copy-start.8
  195.5 1.7 copy-start.9
  225.6 2.6 copy-start
  225.6 2.6 copy-start.10
  225.6 2.8 copy-start.11
  235.5 2.3 copy-start.3
  245.4 47.3 %all-to-all-start.3 = ((f32[32,108,128]{2,1,0:T(8,128)}), f32[32,108,128]{2,1,0:T(8,128)}, u32[]{:S(2)}, u32[]{:S(2)}) async-start(f32[32,108,128]{2,1,0:T(8,128)} %reshape.601), calls=%async_computation.3 | async-start | bytes 3670016 | tf_op jit(solution)/shard_map/all_to_all | solution.py:332
  292.7 47.6 %all-to-all-start.4 = ((f32[32,108,128]{2,1,0:T(8,128)}), f32[32,108,128]{2,1,0:T(8,128)}, u32[]{:S(2)}, u32[]{:S(2)}) async-start(f32[32,108,128]{2,1,0:T(8,128)} %reshape.605), calls=%async_computation.4 | async-start | bytes 3670016 | tf_op jit(solution)/shard_map/all_to_all | solution.py:332
  310.9 3.5 copy-start.7
  340.3 58.3 %all-to-all-start.5 = ((f32[32,108,128]{2,1,0:T(8,128)}), f32[32,108,128]{2,1,0:T(8,128)}, u32[]{:S(2)}, u32[]{:S(2)}) async-start(f32[32,108,128]{2,1,0:T(8,128)} %reshape.609), calls=%async_computation.5 | async-start | bytes 3670016 | tf_op jit(solution)/shard_map/all_to_all | solution.py:332
  344.9 3.1 copy-start.1
  344.9 3.8 copy-start.2
  344.9 4.5 %copy-start.4 = (f32[2,192,6,192]{3,1,2,0:T(8,128)S(1)}, f32[2,192,6,192]{3,1,2,0:T(8,128)}, u32[]{:S(2)}) copy-start(f32[2,192,6,192]{3,1,2,0:T(8,128)} %copy-done.3) | copy-start | bytes 5308420
  354.8 1.2 collective-permute-start.7
  356.0 3.5 collective-permute-start.8
  359.7 3.5 collective-permute-start.9
  363.2 12.5 %collective-permute-start.10 = (f32[2,1,1]{0,2,1:T(1,128)S(1)}, f32[2,1,1]{0,2,1:T(1,128)S(1)}, u32[]{:S(2)}, u32[]{:S(2)}) collective-permute-start(f32[2,1,1]{0,2,1:T(1,128)S(1)} %add.320), channel_id=1, source_target_pairs={{0,8},{1,9},{2,10},{3,11},{4,12},{5,13},{6,14},{7,15},{8,0},{9,1},... | collective-permute-start | bytes 32 | tf_op jit(solution)/shard_map/ppermute | solution.py:238
  375.7 12.3 %collective-permute-start.11 = (f32[2,1,1]{0,2,1:T(1,128)S(1)}, f32[2,1,1]{0,2,1:T(1,128)S(1)}, u32[]{:S(2)}, u32[]{:S(2)}) collective-permute-start(f32[2,1,1]{0,2,1:T(1,128)S(1)} %add.321), channel_id=1, source_target_pairs={{0,16},{1,17},{2,18},{3,19},{4,20},{5,21},{6,22},{7,23},{8,24},{9,... | collective-permute-start | bytes 32 | tf_op jit(solution)/shard_map/ppermute | solution.py:238
  407.3 2.1 copy-start.6
  410.1 0.8 copy-start.13
where the time goes:
time: 425 us; the launch traced here: 418 us
  waiting for transfers between devices  144 us (34%)
  local copies, waits for them, and re-layouts  106 us (25%)
  matrix products  55.6 us (13%)
  starting transfers between devices  48.3 us (11%)
  Pallas kernels  39 us (9%)
  other arithmetic  19.5 us (5%)
  between operations  5.18 us (1%)
    all_to_all x6, waiting for transfers between devices, exchange_rows(): lax.all_to_all(moved, 'wide', split_axis=0, concat_axis=0, tiled=True)  116 us
    pallas_call x3, Pallas kernels, front_pass(): pl.pallas_call(functools.partial(front_kernel, comps), grid=(band_count,...  39 us
    all_to_all x6, starting transfers between devices, exchange_rows(): lax.all_to_all(moved, 'wide', split_axis=0, concat_axis=0, tiled=True)  26.9 us
    dot_general x6, matrix products, transform(): jnp.einsum('pbckyz,pqkn->qbcnyz', stacked, table, precision=three_pass)  24.1 us
    ppermute x5, waiting for transfers between devices, butterfly_sum(): values = values + lax.ppermute(values, axis, pairs)  23.5 us
    reshape x6, local copies, waits for them, and re-layouts, exchange_rows(): moved = jnp.transpose(field, order).reshape(wide_count, -1, 128)  22.5 us
    reshape x6, local copies, waits for them, and re-layouts, exchange_rows(): moved.reshape(wide_count, local_split, bands, comps, field.shape[keep_dim...  21 us
    transpose x6, local copies, waits for them, and re-layouts, exchange_rows(): moved = jnp.transpose(field, order).reshape(wide_count, -1, 128)  20.1 us
  transfers between devices with their start and end apart: 18, of which 14 were waited for; matrix products, arithmetic and copies ran while one was open for 21% of the time, Pallas kernels for 6%

commit v1 on v0

--- a/solution.py
+++ b/solution.py
@@ -365,7 +365,7 @@
     part_im = jnp.einsum("an,bn->ab", left_re, right_im, precision=highest) - jnp.einsum(
         "an,bn->ab", left_im, right_re, precision=highest
     )
-    total_re, total_im = butterfly_sum(jnp.stack([part_re, part_im], axis=0), "wide", wide_count)
+    total_re, total_im = radix_sum(jnp.stack([part_re, part_im], axis=0), "wide", wide_count)
     rayleigh = jnp.stack([total_re * scale_all, total_im * scale_all], axis=0)
     return (applied, rayleigh)
 

time: 425 us -> 425 us (level)
    ppermute x5 -> x0, waiting for transfers between devices: 23.5 us -> none  [butterfly_sum(): values = values + lax.ppermute(values, axis, pairs)]
    ppermute x7 -> x14, waiting for transfers between devices: 5.02 us -> 25.7 us  [radix_sum(): got = lax.ppermute(values, axis, pairs)]
    ppermute x7 -> x14, starting transfers between devices: 11.8 us -> 24.5 us  [radix_sum(): got = lax.ppermute(values, axis, pairs)]
    ppermute x5 -> x0, starting transfers between devices: 9.62 us -> none  [butterfly_sum(): values = values + lax.ppermute(values, axis, pairs)]
  transfers between devices with their start and end apart: 18 -> 20, of which waited for: 14 -> 14; matrix products, arithmetic and copies ran while one was open for 21% -> 21% of each run, Pallas kernels for 6% -> 6%
where the time goes in v1:
time: 425 us; the launch traced here: 418 us
  waiting for transfers between devices  141 us (33%)
  local copies, waits for them, and re-layouts  106 us (25%)
  matrix products  55.6 us (13%)
  starting transfers between devices  51.4 us (12%)
  Pallas kernels  39 us (9%)
  other arithmetic  19.4 us (5%)
  between operations  5.07 us (1%)
    all_to_all x6, waiting for transfers between devices, exchange_rows(): lax.all_to_all(moved, 'wide', split_axis=0, concat_axis=0, tiled=True)  116 us
    pallas_call x3, Pallas kernels, front_pass(): pl.pallas_call(functools.partial(front_kernel, comps), grid=(band_count,...  39 us
    all_to_all x6, starting transfers between devices, exchange_rows(): lax.all_to_all(moved, 'wide', split_axis=0, concat_axis=0, tiled=True)  26.9 us
    ppermute x14, waiting for transfers between devices, radix_sum(): got = lax.ppermute(values, axis, pairs)  25.7 us
    ppermute x14, starting transfers between devices, radix_sum(): got = lax.ppermute(values, axis, pairs)  24.5 us
    dot_general x6, matrix products, transform(): jnp.einsum('pbckyz,pqkn->qbcnyz', stacked, table, precision=three_pass)  24.1 us
    reshape x6, local copies, waits for them, and re-layouts, exchange_rows(): moved = jnp.transpose(field, order).reshape(wide_count, -1, 128)  22.5 us
    reshape x6, local copies, waits for them, and re-layouts, exchange_rows(): moved.reshape(wide_count, local_split, bands, comps, field.shape[keep_dim...  21 us
  transfers between devices with their start and end apart: 20, of which 14 were waited for; matrix products, arithmetic and copies ran while one was open for 21% of the time, Pallas kernels for 6%

profile of v1, /device:TPU:0, one launch (start us, length us, event | category | flops | bytes accessed | tf_op | source)
XLA Modules:
  0.0 417.6 jit_solution(6388088690388123499)
XLA Ops:
  0.6 5.7 %copy.235 = bf16[1,2,3,6,192,192]{5,1,4,3,2,0:T(2,128)(2,1)S(1)} copy(bf16[1,2,3,6,192,192]{5,4,3,2,1,0:T(8,128)(2,1)} %trial_ref.5) | data formatting | bytes 5308416 | tf_op args[0]
  6.3 13.6 %copy.133 = bf16[8,3,6,192,192]{4,0,3,2,1:T(8,128)(2,1)S(1)} copy(bf16[8,3,6,192,192]{4,3,2,1,0:T(8,128)(2,1)} %bitcast.339) | data formatting | bytes 21233664 | tf_op jit(solution)/shard_map/reshape | solution.py:308
  19.9 16.5 %fusion.75 = f32[10,10]{0,1:T(8,128)S(1)} fusion(bf16[2,3,6,192,192]{4,0,3,2,1:T(2,128)(2,1)S(1)} %bitcast.362, bf16[8,3,6,192,192]{4,0,3,2,1:T(8,128)(2,1)S(1)} %copy.133), kind=kOutput, calls=%fused_computation.95 | convolution fusion | flops 159252480 | bytes 13271440 | tf_op jit(solution)/shard_map/icxyz,jcxyz->ij/dot_general | solution.py:312
  49.3 2.7 collective-permute-start.6
  58.5 12.9 %shard_map.168 = f32[2,1,1,6,192,192]{5,4,3,2,1,0:T(8,128)} custom-call(f32[1,8]{1,0:T(1,128)} %fusion.104.coef_ref, f32[6]{0:T(128)} %fusion.119.qx_ref, bf16[1,2,3,6,192,192]{5,4,3,2,1,0:T(8,128)(2,1)} %trial_ref.5, bf16[4,2,3,6,192,192]{5,4,3,2,1,0:T(8,128)(2,1)} %locked_ref.5, bf16[192,192]{1,0:T(8,128)(2,1)} %constant.316.clone.chi_ref, ...), custom_call_target="tpu_custom_call" | custom-call | tf_op jit(solution)/shard_map/pallas_call | solution.py:180
  71.4 3.5 copy.56
  74.9 3.1 reshape.595
  78.0 5.1 %all-to-all-start.1 = ((f32[32,108,128]{2,1,0:T(8,128)}), f32[32,108,128]{2,1,0:T(8,128)}, u32[]{:S(2)}, u32[]{:S(2)}) async-start(f32[32,108,128]{2,1,0:T(8,128)} %reshape.595), calls=%async_computation.1 | async-start | bytes 3670016 | tf_op jit(solution)/shard_map/all_to_all | solution.py:332
  83.2 13.1 %shard_map.167 = f32[2,1,1,6,192,192]{5,4,3,2,1,0:T(8,128)} custom-call(f32[1,8]{1,0:T(1,128)} %fusion.104.coef_ref, f32[6]{0:T(128)} %fusion.119.qx_ref, bf16[1,2,3,6,192,192]{5,4,3,2,1,0:T(8,128)(2,1)} %trial_ref.5, bf16[4,2,3,6,192,192]{5,4,3,2,1,0:T(8,128)(2,1)} %locked_ref.5, bf16[192,192]{1,0:T(8,128)(2,1)} %constant.316.clone.chi_ref, ...), custom_call_target="tpu_custom_call" | custom-call | tf_op jit(solution)/shard_map/pallas_call | solution.py:180
  96.2 3.5 copy.53
  99.7 3.1 reshape.592
  102.9 23.5 %all-to-all-done.1 = f32[32,108,128]{2,1,0:T(8,128)} async-done(((f32[32,108,128]{2,1,0:T(8,128)}), f32[32,108,128]{2,1,0:T(8,128)}, u32[]{:S(2)}, u32[]{:S(2)}) %all-to-all-start.1) | async-done | bytes 1769504 | tf_op jit(solution)/shard_map/all_to_all | solution.py:332
  126.4 4.1 all-to-all-start
  130.5 13.1 %shard_map.169 = f32[2,1,1,6,192,192]{5,4,3,2,1,0:T(8,128)} custom-call(f32[1,8]{1,0:T(1,128)} %fusion.104.coef_ref, f32[6]{0:T(128)} %fusion.119.qx_ref, bf16[1,2,3,6,192,192]{5,4,3,2,1,0:T(8,128)(2,1)} %trial_ref.5, bf16[4,2,3,6,192,192]{5,4,3,2,1,0:T(8,128)(2,1)} %locked_ref.5, bf16[192,192]{1,0:T(8,128)(2,1)} %constant.316.clone.chi_ref, ...), custom_call_target="tpu_custom_call" | custom-call | tf_op jit(solution)/shard_map/pallas_call | solution.py:180
  143.6 3.5 copy.59
  147.1 3.1 reshape.598
  150.2 23.5 %all-to-all-done = f32[32,108,128]{2,1,0:T(8,128)} async-done(((f32[32,108,128]{2,1,0:T(8,128)}), f32[32,108,128]{2,1,0:T(8,128)}, u32[]{:S(2)}, u32[]{:S(2)}) %all-to-all-start) | async-done | bytes 1769504 | tf_op jit(solution)/shard_map/all_to_all | solution.py:332
  173.7 4.5 %all-to-all-start.2 = ((f32[32,108,128]{2,1,0:T(8,128)}), f32[32,108,128]{2,1,0:T(8,128)}, u32[]{:S(2)}, u32[]{:S(2)}) async-start(f32[32,108,128]{2,1,0:T(8,128)} %reshape.598), calls=%async_computation.2 | async-start | bytes 3670016 | tf_op jit(solution)/shard_map/all_to_all | solution.py:332
  187.3 2.9 reshape.596
  192.5 2.9 reshape.593
  199.4 3.6 fusion.33
  203.0 18.5 %all-to-all-done.2 = f32[32,108,128]{2,1,0:T(8,128)} async-done(((f32[32,108,128]{2,1,0:T(8,128)}), f32[32,108,128]{2,1,0:T(8,128)}, u32[]{:S(2)}, u32[]{:S(2)}) %all-to-all-start.2) | async-done | bytes 1769504 | tf_op jit(solution)/shard_map/all_to_all | solution.py:332
  221.5 4.1 reshape.599
  225.6 2.6 copy.60
  228.4 7.1 %fusion.24 = (f32[2,192,6,192]{3,1,2,0:T(8,128)}, f32[2,192,6,192]{3,1,2,0:T(8,128)}, f32[2,192,6,192]{3,1,2,0:T(8,128)S(1)}, f32[2,192,6,192,1]{3,1,4,2,0:T(8,128)}) fusion(f32[2,192,6,192,1]{3,1,4,2,0:T(8,128)S(1)} %fusion.31, f32[2,192,6,192,1]{3,1,4,2,0:T(8,128)S(1)} %copy-done, f32[192,6,192]{2,0,1:T(8,128)} %get-tuple-element.20, ...), kind=kOutput, calls=%fused_computation.43 | convolution fusion | flops 1025998848 | bytes 18284544 | tf_op jit(solution)/shard_map/pbckyz,pqkn->qbcnyz/dot_general | solution.py:80
  237.7 3.2 copy.64
  241.0 4.4 %reshape.601 = f32[32,108,128]{2,1,0:T(8,128)} reshape(f32[192,1,1,6,2,192]{5,4,3,0,2,1:T(2,128)} %copy.64) | data formatting | bytes 3538944 | tf_op jit(solution)/shard_map/reshape | solution.py:331
  245.4 4.1 all-to-all-start.3
  249.5 3.7 fusion.57
  253.2 3.2 copy.72
  256.5 4.4 %reshape.605 = f32[32,108,128]{2,1,0:T(8,128)} reshape(f32[192,1,1,6,2,192]{5,4,3,0,2,1:T(2,128)} %copy.72) | data formatting | bytes 3538944 | tf_op jit(solution)/shard_map/reshape | solution.py:331
  260.8 31.9 %all-to-all-done.3 = f32[32,108,128]{2,1,0:T(8,128)} async-done(((f32[32,108,128]{2,1,0:T(8,128)}), f32[32,108,128]{2,1,0:T(8,128)}, u32[]{:S(2)}, u32[]{:S(2)}) %all-to-all-start.3) | async-done | bytes 1769504 | tf_op jit(solution)/shard_map/all_to_all | solution.py:332
  292.7 4.4 %all-to-all-start.4 = ((f32[32,108,128]{2,1,0:T(8,128)}), f32[32,108,128]{2,1,0:T(8,128)}, u32[]{:S(2)}, u32[]{:S(2)}) async-start(f32[32,108,128]{2,1,0:T(8,128)} %reshape.605), calls=%async_computation.4 | async-start | bytes 3670016 | tf_op jit(solution)/shard_map/all_to_all | solution.py:332
  297.1 5.2 %fusion.66 = f32[2,1,1,192,6,192]{5,3,4,0,2,1:T(8,128)} fusion(f32[2,192,6,192]{3,1,2,0:T(8,128)} %get-tuple-element.15, f32[1,2,192,192]{2,3,1,0:T(8,128)S(1)} %get-tuple-element.34, f32[1,2,192,192]{2,3,1,0:T(8,128)S(1)} %get-tuple-element.31), kind=kOutput, calls=%fused_computation.80 | convolution fusion | flops 1019363328 | bytes 4128768 | tf_op jit(solution)/shard_map/pbckyz,pqkn->qbcnyz/dot_general | solution.py:80
  302.2 3.9 reshape.602
  310.9 3.5 fusion.54
  314.4 3.3 copy.80
  317.6 4.4 %reshape.609 = f32[32,108,128]{2,1,0:T(8,128)} reshape(f32[192,1,1,6,2,192]{5,4,3,0,2,1:T(2,128)} %copy.80) | data formatting | bytes 3538944 | tf_op jit(solution)/shard_map/reshape | solution.py:331
  322.0 18.3 %all-to-all-done.4 = f32[32,108,128]{2,1,0:T(8,128)} async-done(((f32[32,108,128]{2,1,0:T(8,128)}), f32[32,108,128]{2,1,0:T(8,128)}, u32[]{:S(2)}, u32[]{:S(2)}) %all-to-all-start.4) | async-done | bytes 1769504 | tf_op jit(solution)/shard_map/all_to_all | solution.py:332
  340.3 4.5 %all-to-all-start.5 = ((f32[32,108,128]{2,1,0:T(8,128)}), f32[32,108,128]{2,1,0:T(8,128)}, u32[]{:S(2)}, u32[]{:S(2)}) async-start(f32[32,108,128]{2,1,0:T(8,128)} %reshape.609), calls=%async_computation.5 | async-start | bytes 3670016 | tf_op jit(solution)/shard_map/all_to_all | solution.py:332
  344.9 3.0 pad_maximum_fusion.1
  363.7 3.1 collective-permute-done.10
  366.8 8.9 %collective-permute-done.11 = f32[2,1,1]{0,2,1:T(1,128)S(1)} collective-permute-done((f32[2,1,1]{0,2,1:T(1,128)S(1)}, f32[2,1,1]{0,2,1:T(1,128)S(1)}, u32[]{:S(2)}, u32[]{:S(2)}) %collective-permute-start.11) | collective-permute-done | bytes 40 | tf_op jit(solution)/shard_map/ppermute | solution.py:216
  375.7 5.0 %collective-permute-start.13 = (f32[2,1,1]{0,2,1:T(1,128)S(1)}, f32[2,1,1]{0,2,1:T(1,128)S(1)}, u32[]{:S(2)}, u32[]{:S(2)}) collective-permute-start(f32[2,1,1]{0,2,1:T(1,128)S(1)} %fusion.114), channel_id=1, source_target_pairs={{16,0},{17,1},{18,2},{19,3},{20,4},{21,5},{22,6},{23,7},{24,8},{25... | collective-permute-start | bytes 32 | tf_op jit(solution)/shard_map/ppermute | solution.py:216
  380.7 7.3 %collective-permute-done.13 = f32[2,1,1]{0,2,1:T(1,128)S(1)} collective-permute-done((f32[2,1,1]{0,2,1:T(1,128)S(1)}, f32[2,1,1]{0,2,1:T(1,128)S(1)}, u32[]{:S(2)}, u32[]{:S(2)}) %collective-permute-start.13) | collective-permute-done | bytes 40 | tf_op jit(solution)/shard_map/ppermute | solution.py:216
  390.5 2.9 reshape.606
  398.6 4.1 reshape.610
  413.7 3.7 copy.87
  (108 shorter events, 72.1 us)
Async XLA Ops:
  36.5 5.0 %collective-permute-start = (f32[10,10]{0,1:T(8,128)S(1)}, f32[10,10]{0,1:T(8,128)S(1)}, u32[]{:S(2)}, u32[]{:S(2)}) collective-permute-start(f32[10,10]{0,1:T(8,128)S(1)} %fusion.75), channel_id=1, source_target_pairs={{3,0},{0,1},{1,2},{2,3},{7,4},{4,5},{5,6},{6,7},{11,8},{8,9},{9,10... | collective-permute-start | bytes 1208 | tf_op jit(solution)/shard_map/ppermute | solution.py:216
  37.0 4.5 %collective-permute-start.1 = (f32[10,10]{0,1:T(8,128)S(1)}, f32[10,10]{0,1:T(8,128)S(1)}, u32[]{:S(2)}, u32[]{:S(2)}) collective-permute-start(f32[10,10]{0,1:T(8,128)S(1)} %fusion.75), channel_id=1, source_target_pairs={{2,0},{3,1},{0,2},{1,3},{6,4},{7,5},{4,6},{5,7},{10,8},{11,9},{8,1... | collective-permute-start | bytes 1208 | tf_op jit(solution)/shard_map/ppermute | solution.py:216
  39.5 2.8 collective-permute-start.2
  42.3 4.7 %collective-permute-start.3 = (f32[10,10]{0,1:T(8,128)S(1)}, f32[10,10]{0,1:T(8,128)S(1)}, u32[]{:S(2)}, u32[]{:S(2)}) collective-permute-start(f32[10,10]{0,1:T(8,128)S(1)} %select_add_fusion.2), channel_id=1, source_target_pairs={{12,0},{13,1},{14,2},{15,3},{0,4},{1,5},{2,6},{3,7},{4,8},{5,9},{6... | collective-permute-start | bytes 1208 | tf_op jit(solution)/shard_map/ppermute | solution.py:216
  43.9 3.7 collective-permute-start.4
  45.4 3.8 collective-permute-start.5
  49.3 4.6 %collective-permute-start.6 = (f32[10,10]{0,1:T(8,128)S(1)}, f32[10,10]{0,1:T(8,128)S(1)}, u32[]{:S(2)}, u32[]{:S(2)}) collective-permute-start(f32[10,10]{0,1:T(8,128)S(1)} %select_add_fusion.1), channel_id=1, source_target_pairs={{16,0},{17,1},{18,2},{19,3},{20,4},{21,5},{22,6},{23,7},{24,8},{25... | collective-permute-start | bytes 1208 | tf_op jit(solution)/shard_map/ppermute | solution.py:216
  78.0 48.4 %all-to-all-start.1 = ((f32[32,108,128]{2,1,0:T(8,128)}), f32[32,108,128]{2,1,0:T(8,128)}, u32[]{:S(2)}, u32[]{:S(2)}) async-start(f32[32,108,128]{2,1,0:T(8,128)} %reshape.595), calls=%async_computation.1 | async-start | bytes 3670016 | tf_op jit(solution)/shard_map/all_to_all | solution.py:332
  126.4 47.4 %all-to-all-start = ((f32[32,108,128]{2,1,0:T(8,128)}), f32[32,108,128]{2,1,0:T(8,128)}, u32[]{:S(2)}, u32[]{:S(2)}) async-start(f32[32,108,128]{2,1,0:T(8,128)} %reshape.592), calls=%async_computation | async-start | bytes 3670016 | tf_op jit(solution)/shard_map/all_to_all | solution.py:332
  173.7 47.8 %all-to-all-start.2 = ((f32[32,108,128]{2,1,0:T(8,128)}), f32[32,108,128]{2,1,0:T(8,128)}, u32[]{:S(2)}, u32[]{:S(2)}) async-start(f32[32,108,128]{2,1,0:T(8,128)} %reshape.598), calls=%async_computation.2 | async-start | bytes 3670016 | tf_op jit(solution)/shard_map/all_to_all | solution.py:332
  178.3 3.3 copy-start.5
  181.6 3.3 copy-start.12
  195.5 1.7 copy-start.8
  195.5 1.7 copy-start.9
  225.6 2.6 copy-start
  225.6 2.6 copy-start.10
  225.6 2.8 copy-start.11
  235.5 2.3 copy-start.3
  245.4 47.4 %all-to-all-start.3 = ((f32[32,108,128]{2,1,0:T(8,128)}), f32[32,108,128]{2,1,0:T(8,128)}, u32[]{:S(2)}, u32[]{:S(2)}) async-start(f32[32,108,128]{2,1,0:T(8,128)} %reshape.601), calls=%async_computation.3 | async-start | bytes 3670016 | tf_op jit(solution)/shard_map/all_to_all | solution.py:332
  292.7 47.6 %all-to-all-start.4 = ((f32[32,108,128]{2,1,0:T(8,128)}), f32[32,108,128]{2,1,0:T(8,128)}, u32[]{:S(2)}, u32[]{:S(2)}) async-start(f32[32,108,128]{2,1,0:T(8,128)} %reshape.605), calls=%async_computation.4 | async-start | bytes 3670016 | tf_op jit(solution)/shard_map/all_to_all | solution.py:332
  310.9 3.5 copy-start.7
  340.3 58.3 %all-to-all-start.5 = ((f32[32,108,128]{2,1,0:T(8,128)}), f32[32,108,128]{2,1,0:T(8,128)}, u32[]{:S(2)}, u32[]{:S(2)}) async-start(f32[32,108,128]{2,1,0:T(8,128)} %reshape.609), calls=%async_computation.5 | async-start | bytes 3670016 | tf_op jit(solution)/shard_map/all_to_all | solution.py:332
  344.8 3.1 copy-start.1
  344.8 3.8 copy-start.2
  344.9 4.5 %copy-start.4 = (f32[2,192,6,192]{3,1,2,0:T(8,128)S(1)}, f32[2,192,6,192]{3,1,2,0:T(8,128)}, u32[]{:S(2)}) copy-start(f32[2,192,6,192]{3,1,2,0:T(8,128)} %copy-done.3) | copy-start | bytes 5308420
  354.6 3.4 collective-permute-start.7
  355.0 3.5 collective-permute-start.8
  356.6 2.6 collective-permute-start.9
  359.3 7.5 %collective-permute-start.10 = (f32[2,1,1]{0,2,1:T(1,128)S(1)}, f32[2,1,1]{0,2,1:T(1,128)S(1)}, u32[]{:S(2)}, u32[]{:S(2)}) collective-permute-start(f32[2,1,1]{0,2,1:T(1,128)S(1)} %fusion.117), channel_id=1, source_target_pairs={{12,0},{13,1},{14,2},{15,3},{0,4},{1,5},{2,6},{3,7},{4,8},{5,9},{6... | collective-permute-start | bytes 32 | tf_op jit(solution)/shard_map/ppermute | solution.py:216
  360.8 14.9 %collective-permute-start.11 = (f32[2,1,1]{0,2,1:T(1,128)S(1)}, f32[2,1,1]{0,2,1:T(1,128)S(1)}, u32[]{:S(2)}, u32[]{:S(2)}) collective-permute-start(f32[2,1,1]{0,2,1:T(1,128)S(1)} %fusion.117), channel_id=1, source_target_pairs={{8,0},{9,1},{10,2},{11,3},{12,4},{13,5},{14,6},{15,7},{0,8},{1,9},... | collective-permute-start | bytes 32 | tf_op jit(solution)/shard_map/ppermute | solution.py:216
  362.3 13.5 %collective-permute-start.12 = (f32[2,1,1]{0,2,1:T(1,128)S(1)}, f32[2,1,1]{0,2,1:T(1,128)S(1)}, u32[]{:S(2)}, u32[]{:S(2)}) collective-permute-start(f32[2,1,1]{0,2,1:T(1,128)S(1)} %fusion.117), channel_id=1, source_target_pairs={{4,0},{5,1},{6,2},{7,3},{8,4},{9,5},{10,6},{11,7},{12,8},{13,9},{1... | collective-permute-start | bytes 32 | tf_op jit(solution)/shard_map/ppermute | solution.py:216
  375.7 12.3 %collective-permute-start.13 = (f32[2,1,1]{0,2,1:T(1,128)S(1)}, f32[2,1,1]{0,2,1:T(1,128)S(1)}, u32[]{:S(2)}, u32[]{:S(2)}) collective-permute-start(f32[2,1,1]{0,2,1:T(1,128)S(1)} %fusion.114), channel_id=1, source_target_pairs={{16,0},{17,1},{18,2},{19,3},{20,4},{21,5},{22,6},{23,7},{24,8},{25... | collective-permute-start | bytes 32 | tf_op jit(solution)/shard_map/ppermute | solution.py:216
  407.3 2.1 copy-start.6
  410.1 0.8 copy-start.13

commit v2 on v1

--- a/solution.py
+++ b/solution.py
@@ -201,7 +201,7 @@
     me = lax.axis_index(axis)
     stride = 1
     while stride < count:
-        radix = 4 if count // stride >= 4 else 2
+        radix = min(8, count // stride)
         digit = (me // stride) % radix
         slots = [None] * radix
         for offset in range(radix):

time: 425 us -> 427 us (level)
    ppermute x14 -> x20, starting transfers between devices: 24.5 us -> 29.6 us  [radix_sum(): got = lax.ppermute(values, axis, pairs)]
    ppermute x14 -> x20, waiting for transfers between devices: 25.7 us -> 22.9 us  [radix_sum(): got = lax.ppermute(values, axis, pairs)]
  transfers between devices with their start and end apart: 20 -> 26, of which waited for: 14 -> 11; matrix products, arithmetic and copies ran while one was open for 21% -> 21% of each run, Pallas kernels for 6% -> 6%
where the time goes in v2:
time: 427 us; the launch traced here: 419 us
  waiting for transfers between devices  139 us (33%)
  local copies, waits for them, and re-layouts  106 us (25%)
  matrix products  55.6 us (13%)
  starting transfers between devices  55.3 us (13%)
  Pallas kernels  39 us (9%)
  other arithmetic  19.5 us (5%)
  between operations  5.17 us (1%)
    all_to_all x6, waiting for transfers between devices, exchange_rows(): lax.all_to_all(moved, 'wide', split_axis=0, concat_axis=0, tiled=True)  116 us
    pallas_call x3, Pallas kernels, front_pass(): pl.pallas_call(functools.partial(front_kernel, comps), grid=(band_count,...  39 us
    ppermute x20, starting transfers between devices, radix_sum(): got = lax.ppermute(values, axis, pairs)  29.6 us
    all_to_all x6, starting transfers between devices, exchange_rows(): lax.all_to_all(moved, 'wide', split_axis=0, concat_axis=0, tiled=True)  25.7 us
    dot_general x6, matrix products, transform(): jnp.einsum('pbckyz,pqkn->qbcnyz', stacked, table, precision=three_pass)  24.1 us
    ppermute x20, waiting for transfers between devices, radix_sum(): got = lax.ppermute(values, axis, pairs)  22.9 us
    reshape x6, local copies, waits for them, and re-layouts, exchange_rows(): moved = jnp.transpose(field, order).reshape(wide_count, -1, 128)  22.5 us
    reshape x6, local copies, waits for them, and re-layouts, exchange_rows(): moved.reshape(wide_count, local_split, bands, comps, field.shape[keep_dim...  21 us
  transfers between devices with their start and end apart: 26, of which 11 were waited for; matrix products, arithmetic and copies ran while one was open for 21% of the time, Pallas kernels for 6%

profile of v2, /device:TPU:0, one launch (start us, length us, event | category | flops | bytes accessed | tf_op | source)
XLA Modules:
  0.0 418.9 jit_solution(12784848513254793324)
XLA Ops:
  0.6 5.7 %copy.235 = bf16[1,2,3,6,192,192]{5,1,4,3,2,0:T(2,128)(2,1)S(1)} copy(bf16[1,2,3,6,192,192]{5,4,3,2,1,0:T(8,128)(2,1)} %trial_ref.5) | data formatting | bytes 5308416 | tf_op args[0]
  6.3 13.6 %copy.133 = bf16[8,3,6,192,192]{4,0,3,2,1:T(8,128)(2,1)S(1)} copy(bf16[8,3,6,192,192]{4,3,2,1,0:T(8,128)(2,1)} %bitcast.339) | data formatting | bytes 21233664 | tf_op jit(solution)/shard_map/reshape | solution.py:308
  19.9 16.5 %fusion.75 = f32[10,10]{0,1:T(8,128)S(1)} fusion(bf16[2,3,6,192,192]{4,0,3,2,1:T(2,128)(2,1)S(1)} %bitcast.362, bf16[8,3,6,192,192]{4,0,3,2,1:T(8,128)(2,1)S(1)} %copy.133), kind=kOutput, calls=%fused_computation.95 | convolution fusion | flops 159252480 | bytes 13271440 | tf_op jit(solution)/shard_map/icxyz,jcxyz->ij/dot_general | solution.py:312
  37.0 2.6 collective-permute-start.1
  49.9 2.6 collective-permute-start.8
  61.0 12.9 %shard_map.168 = f32[2,1,1,6,192,192]{5,4,3,2,1,0:T(8,128)} custom-call(f32[1,8]{1,0:T(1,128)} %fusion.104.coef_ref, f32[6]{0:T(128)} %fusion.122.qx_ref, bf16[1,2,3,6,192,192]{5,4,3,2,1,0:T(8,128)(2,1)} %trial_ref.5, bf16[4,2,3,6,192,192]{5,4,3,2,1,0:T(8,128)(2,1)} %locked_ref.5, bf16[192,192]{1,0:T(8,128)(2,1)} %constant.478.clone.chi_ref, ...), custom_call_target="tpu_custom_call" | custom-call | tf_op jit(solution)/shard_map/pallas_call | solution.py:180
  73.9 3.5 copy.56
  77.4 3.1 reshape.595
  80.5 4.0 all-to-all-start.1
  84.5 13.1 %shard_map.167 = f32[2,1,1,6,192,192]{5,4,3,2,1,0:T(8,128)} custom-call(f32[1,8]{1,0:T(1,128)} %fusion.104.coef_ref, f32[6]{0:T(128)} %fusion.122.qx_ref, bf16[1,2,3,6,192,192]{5,4,3,2,1,0:T(8,128)(2,1)} %trial_ref.5, bf16[4,2,3,6,192,192]{5,4,3,2,1,0:T(8,128)(2,1)} %locked_ref.5, bf16[192,192]{1,0:T(8,128)(2,1)} %constant.478.clone.chi_ref, ...), custom_call_target="tpu_custom_call" | custom-call | tf_op jit(solution)/shard_map/pallas_call | solution.py:180
  97.6 3.5 copy.53
  101.0 3.1 reshape.592
  104.2 23.5 %all-to-all-done.1 = f32[32,108,128]{2,1,0:T(8,128)} async-done(((f32[32,108,128]{2,1,0:T(8,128)}), f32[32,108,128]{2,1,0:T(8,128)}, u32[]{:S(2)}, u32[]{:S(2)}) %all-to-all-start.1) | async-done | bytes 1769504 | tf_op jit(solution)/shard_map/all_to_all | solution.py:332
  127.7 4.1 all-to-all-start
  131.9 13.1 %shard_map.169 = f32[2,1,1,6,192,192]{5,4,3,2,1,0:T(8,128)} custom-call(f32[1,8]{1,0:T(1,128)} %fusion.104.coef_ref, f32[6]{0:T(128)} %fusion.122.qx_ref, bf16[1,2,3,6,192,192]{5,4,3,2,1,0:T(8,128)(2,1)} %trial_ref.5, bf16[4,2,3,6,192,192]{5,4,3,2,1,0:T(8,128)(2,1)} %locked_ref.5, bf16[192,192]{1,0:T(8,128)(2,1)} %constant.478.clone.chi_ref, ...), custom_call_target="tpu_custom_call" | custom-call | tf_op jit(solution)/shard_map/pallas_call | solution.py:180
  144.9 3.5 copy.59
  148.4 3.1 reshape.598
  151.5 23.5 %all-to-all-done = f32[32,108,128]{2,1,0:T(8,128)} async-done(((f32[32,108,128]{2,1,0:T(8,128)}), f32[32,108,128]{2,1,0:T(8,128)}, u32[]{:S(2)}, u32[]{:S(2)}) %all-to-all-start) | async-done | bytes 1769504 | tf_op jit(solution)/shard_map/all_to_all | solution.py:332
  175.1 4.6 %all-to-all-start.2 = ((f32[32,108,128]{2,1,0:T(8,128)}), f32[32,108,128]{2,1,0:T(8,128)}, u32[]{:S(2)}, u32[]{:S(2)}) async-start(f32[32,108,128]{2,1,0:T(8,128)} %reshape.598), calls=%async_computation.2 | async-start | bytes 3670016 | tf_op jit(solution)/shard_map/all_to_all | solution.py:332
  188.7 2.9 reshape.596
  193.9 2.9 reshape.593
  200.7 3.6 fusion.33
  204.3 18.5 %all-to-all-done.2 = f32[32,108,128]{2,1,0:T(8,128)} async-done(((f32[32,108,128]{2,1,0:T(8,128)}), f32[32,108,128]{2,1,0:T(8,128)}, u32[]{:S(2)}, u32[]{:S(2)}) %all-to-all-start.2) | async-done | bytes 1769504 | tf_op jit(solution)/shard_map/all_to_all | solution.py:332
  222.9 4.1 reshape.599
  227.0 2.6 copy.60
  229.8 7.1 %fusion.24 = (f32[2,192,6,192]{3,1,2,0:T(8,128)}, f32[2,192,6,192]{3,1,2,0:T(8,128)}, f32[2,192,6,192]{3,1,2,0:T(8,128)S(1)}, f32[2,192,6,192,1]{3,1,4,2,0:T(8,128)}) fusion(f32[2,192,6,192,1]{3,1,4,2,0:T(8,128)S(1)} %fusion.31, f32[2,192,6,192,1]{3,1,4,2,0:T(8,128)S(1)} %copy-done, f32[192,6,192]{2,0,1:T(8,128)} %get-tuple-element.20, ...), kind=kOutput, calls=%fused_computation.43 | convolution fusion | flops 1025998848 | bytes 18284544 | tf_op jit(solution)/shard_map/pbckyz,pqkn->qbcnyz/dot_general | solution.py:80
  239.1 3.2 copy.64
  242.3 4.4 %reshape.601 = f32[32,108,128]{2,1,0:T(8,128)} reshape(f32[192,1,1,6,2,192]{5,4,3,0,2,1:T(2,128)} %copy.64) | data formatting | bytes 3538944 | tf_op jit(solution)/shard_map/reshape | solution.py:331
  246.7 4.1 all-to-all-start.3
  250.8 3.7 fusion.57
  254.6 3.2 copy.72
  257.8 4.4 %reshape.605 = f32[32,108,128]{2,1,0:T(8,128)} reshape(f32[192,1,1,6,2,192]{5,4,3,0,2,1:T(2,128)} %copy.72) | data formatting | bytes 3538944 | tf_op jit(solution)/shard_map/reshape | solution.py:331
  262.2 31.9 %all-to-all-done.3 = f32[32,108,128]{2,1,0:T(8,128)} async-done(((f32[32,108,128]{2,1,0:T(8,128)}), f32[32,108,128]{2,1,0:T(8,128)}, u32[]{:S(2)}, u32[]{:S(2)}) %all-to-all-start.3) | async-done | bytes 1769504 | tf_op jit(solution)/shard_map/all_to_all | solution.py:332
  294.0 4.4 %all-to-all-start.4 = ((f32[32,108,128]{2,1,0:T(8,128)}), f32[32,108,128]{2,1,0:T(8,128)}, u32[]{:S(2)}, u32[]{:S(2)}) async-start(f32[32,108,128]{2,1,0:T(8,128)} %reshape.605), calls=%async_computation.4 | async-start | bytes 3670016 | tf_op jit(solution)/shard_map/all_to_all | solution.py:332
  298.4 5.2 %fusion.66 = f32[2,1,1,192,6,192]{5,3,4,0,2,1:T(8,128)} fusion(f32[2,192,6,192]{3,1,2,0:T(8,128)} %get-tuple-element.15, f32[1,2,192,192]{2,3,1,0:T(8,128)S(1)} %get-tuple-element.34, f32[1,2,192,192]{2,3,1,0:T(8,128)S(1)} %get-tuple-element.31), kind=kOutput, calls=%fused_computation.80 | convolution fusion | flops 1019363328 | bytes 4128768 | tf_op jit(solution)/shard_map/pbckyz,pqkn->qbcnyz/dot_general | solution.py:80
  303.6 3.9 reshape.602
  312.2 3.5 fusion.54
  315.7 3.3 copy.80
  319.0 4.4 %reshape.609 = f32[32,108,128]{2,1,0:T(8,128)} reshape(f32[192,1,1,6,2,192]{5,4,3,0,2,1:T(2,128)} %copy.80) | data formatting | bytes 3538944 | tf_op jit(solution)/shard_map/reshape | solution.py:331
  323.4 18.2 %all-to-all-done.4 = f32[32,108,128]{2,1,0:T(8,128)} async-done(((f32[32,108,128]{2,1,0:T(8,128)}), f32[32,108,128]{2,1,0:T(8,128)}, u32[]{:S(2)}, u32[]{:S(2)}) %all-to-all-start.4) | async-done | bytes 1769504 | tf_op jit(solution)/shard_map/all_to_all | solution.py:332
  341.6 4.5 %all-to-all-start.5 = ((f32[32,108,128]{2,1,0:T(8,128)}), f32[32,108,128]{2,1,0:T(8,128)}, u32[]{:S(2)}, u32[]{:S(2)}) async-start(f32[32,108,128]{2,1,0:T(8,128)} %reshape.609), calls=%async_computation.5 | async-start | bytes 3670016 | tf_op jit(solution)/shard_map/all_to_all | solution.py:332
  346.2 3.0 pad_maximum_fusion.1
  371.4 8.9 %collective-permute-done.17 = f32[2,1,1]{0,2,1:T(1,128)S(1)} collective-permute-done((f32[2,1,1]{0,2,1:T(1,128)S(1)}, f32[2,1,1]{0,2,1:T(1,128)S(1)}, u32[]{:S(2)}, u32[]{:S(2)}) %collective-permute-start.17) | collective-permute-done | bytes 40 | tf_op jit(solution)/shard_map/ppermute | solution.py:216
  380.3 9.1 %collective-permute-done.18 = f32[2,1,1]{0,2,1:T(1,128)S(1)} collective-permute-done((f32[2,1,1]{0,2,1:T(1,128)S(1)}, f32[2,1,1]{0,2,1:T(1,128)S(1)}, u32[]{:S(2)}, u32[]{:S(2)}) %collective-permute-start.18) | collective-permute-done | bytes 40 | tf_op jit(solution)/shard_map/ppermute | solution.py:216
  391.9 2.9 reshape.606
  399.9 4.1 reshape.610
  404.0 2.5 copy.81
  415.0 3.7 copy.87
  (118 shorter events, 75.8 us)
Async XLA Ops:
  36.5 6.6 %collective-permute-start = (f32[10,10]{0,1:T(8,128)S(1)}, f32[10,10]{0,1:T(8,128)S(1)}, u32[]{:S(2)}, u32[]{:S(2)}) collective-permute-start(f32[10,10]{0,1:T(8,128)S(1)} %fusion.75), channel_id=1, source_target_pairs={{7,0},{0,1},{1,2},{2,3},{3,4},{4,5},{5,6},{6,7},{15,8},{8,9},{9,10... | collective-permute-start | bytes 1208 | tf_op jit(solution)/shard_map/ppermute | solution.py:216
  37.0 7.6 %collective-permute-start.1 = (f32[10,10]{0,1:T(8,128)S(1)}, f32[10,10]{0,1:T(8,128)S(1)}, u32[]{:S(2)}, u32[]{:S(2)}) collective-permute-start(f32[10,10]{0,1:T(8,128)S(1)} %fusion.75), channel_id=1, source_target_pairs={{6,0},{7,1},{0,2},{1,3},{2,4},{3,5},{4,6},{5,7},{14,8},{15,9},{8,1... | collective-permute-start | bytes 1208 | tf_op jit(solution)/shard_map/ppermute | solution.py:216
  39.5 7.3 %collective-permute-start.2 = (f32[10,10]{0,1:T(8,128)S(1)}, f32[10,10]{0,1:T(8,128)S(1)}, u32[]{:S(2)}, u32[]{:S(2)}) collective-permute-start(f32[10,10]{0,1:T(8,128)S(1)} %fusion.75), channel_id=1, source_target_pairs={{5,0},{6,1},{7,2},{0,3},{1,4},{2,5},{3,6},{4,7},{13,8},{14,9},{15,... | collective-permute-start | bytes 1208 | tf_op jit(solution)/shard_map/ppermute | solution.py:216
  41.9 5.0 %collective-permute-start.3 = (f32[10,10]{0,1:T(8,128)S(1)}, f32[10,10]{0,1:T(8,128)S(1)}, u32[]{:S(2)}, u32[]{:S(2)}) collective-permute-start(f32[10,10]{0,1:T(8,128)S(1)} %fusion.75), channel_id=1, source_target_pairs={{4,0},{5,1},{6,2},{7,3},{0,4},{1,5},{2,6},{3,7},{12,8},{13,9},{14,... | collective-permute-start | bytes 1208 | tf_op jit(solution)/shard_map/ppermute | solution.py:216
  42.4 4.5 %collective-permute-start.4 = (f32[10,10]{0,1:T(8,128)S(1)}, f32[10,10]{0,1:T(8,128)S(1)}, u32[]{:S(2)}, u32[]{:S(2)}) collective-permute-start(f32[10,10]{0,1:T(8,128)S(1)} %fusion.75), channel_id=1, source_target_pairs={{3,0},{4,1},{5,2},{6,3},{7,4},{0,5},{1,6},{2,7},{11,8},{12,9},{13,... | collective-permute-start | bytes 1208 | tf_op jit(solution)/shard_map/ppermute | solution.py:216
  43.1 3.8 collective-permute-start.5
  44.5 3.7 collective-permute-start.6
  48.3 5.8 %collective-permute-start.7 = (f32[10,10]{0,1:T(8,128)S(1)}, f32[10,10]{0,1:T(8,128)S(1)}, u32[]{:S(2)}, u32[]{:S(2)}) collective-permute-start(f32[10,10]{0,1:T(8,128)S(1)} %select_add_fusion.1), channel_id=1, source_target_pairs={{24,0},{25,1},{26,2},{27,3},{28,4},{29,5},{30,6},{31,7},{0,8},{1,9... | collective-permute-start | bytes 1208 | tf_op jit(solution)/shard_map/ppermute | solution.py:216
  49.9 4.6 %collective-permute-start.8 = (f32[10,10]{0,1:T(8,128)S(1)}, f32[10,10]{0,1:T(8,128)S(1)}, u32[]{:S(2)}, u32[]{:S(2)}) collective-permute-start(f32[10,10]{0,1:T(8,128)S(1)} %select_add_fusion.1), channel_id=1, source_target_pairs={{16,0},{17,1},{18,2},{19,3},{20,4},{21,5},{22,6},{23,7},{24,8},{25... | collective-permute-start | bytes 1208 | tf_op jit(solution)/shard_map/ppermute | solution.py:216
  52.5 3.8 collective-permute-start.9
  80.5 47.2 %all-to-all-start.1 = ((f32[32,108,128]{2,1,0:T(8,128)}), f32[32,108,128]{2,1,0:T(8,128)}, u32[]{:S(2)}, u32[]{:S(2)}) async-start(f32[32,108,128]{2,1,0:T(8,128)} %reshape.595), calls=%async_computation.1 | async-start | bytes 3670016 | tf_op jit(solution)/shard_map/all_to_all | solution.py:332
  127.7 47.4 %all-to-all-start = ((f32[32,108,128]{2,1,0:T(8,128)}), f32[32,108,128]{2,1,0:T(8,128)}, u32[]{:S(2)}, u32[]{:S(2)}) async-start(f32[32,108,128]{2,1,0:T(8,128)} %reshape.592), calls=%async_computation | async-start | bytes 3670016 | tf_op jit(solution)/shard_map/all_to_all | solution.py:332
  175.1 47.8 %all-to-all-start.2 = ((f32[32,108,128]{2,1,0:T(8,128)}), f32[32,108,128]{2,1,0:T(8,128)}, u32[]{:S(2)}, u32[]{:S(2)}) async-start(f32[32,108,128]{2,1,0:T(8,128)} %reshape.598), calls=%async_computation.2 | async-start | bytes 3670016 | tf_op jit(solution)/shard_map/all_to_all | solution.py:332
  179.7 3.3 copy-start.5
  183.0 3.3 copy-start.12
  196.8 1.7 copy-start.8
  196.8 1.7 copy-start.9
  227.0 2.6 copy-start
  227.0 2.6 copy-start.10
  227.0 2.8 copy-start.11
  236.9 2.3 copy-start.3
  246.7 47.3 %all-to-all-start.3 = ((f32[32,108,128]{2,1,0:T(8,128)}), f32[32,108,128]{2,1,0:T(8,128)}, u32[]{:S(2)}, u32[]{:S(2)}) async-start(f32[32,108,128]{2,1,0:T(8,128)} %reshape.601), calls=%async_computation.3 | async-start | bytes 3670016 | tf_op jit(solution)/shard_map/all_to_all | solution.py:332
  294.0 47.6 %all-to-all-start.4 = ((f32[32,108,128]{2,1,0:T(8,128)}), f32[32,108,128]{2,1,0:T(8,128)}, u32[]{:S(2)}, u32[]{:S(2)}) async-start(f32[32,108,128]{2,1,0:T(8,128)} %reshape.605), calls=%async_computation.4 | async-start | bytes 3670016 | tf_op jit(solution)/shard_map/all_to_all | solution.py:332
  312.2 3.5 copy-start.7
  341.6 58.3 %all-to-all-start.5 = ((f32[32,108,128]{2,1,0:T(8,128)}), f32[32,108,128]{2,1,0:T(8,128)}, u32[]{:S(2)}, u32[]{:S(2)}) async-start(f32[32,108,128]{2,1,0:T(8,128)} %reshape.609), calls=%async_computation.5 | async-start | bytes 3670016 | tf_op jit(solution)/shard_map/all_to_all | solution.py:332
  346.2 3.1 copy-start.1
  346.2 3.8 copy-start.2
  346.2 4.5 %copy-start.4 = (f32[2,192,6,192]{3,1,2,0:T(8,128)S(1)}, f32[2,192,6,192]{3,1,2,0:T(8,128)}, u32[]{:S(2)}) copy-start(f32[2,192,6,192]{3,1,2,0:T(8,128)} %copy-done.3) | copy-start | bytes 5308420
  356.0 5.0 %collective-permute-start.10 = (f32[2,1,1]{0,2,1:T(1,128)S(1)}, f32[2,1,1]{0,2,1:T(1,128)S(1)}, u32[]{:S(2)}, u32[]{:S(2)}) collective-permute-start(f32[2,1,1]{0,2,1:T(1,128)S(1)} %pad_maximum_fusion.8), channel_id=1, source_target_pairs={{7,0},{0,1},{1,2},{2,3},{3,4},{4,5},{5,6},{6,7},{15,8},{8,9},{9,10... | collective-permute-start | bytes 32 | tf_op jit(solution)/shard_map/ppermute | solution.py:216
  356.4 6.1 %collective-permute-start.11 = (f32[2,1,1]{0,2,1:T(1,128)S(1)}, f32[2,1,1]{0,2,1:T(1,128)S(1)}, u32[]{:S(2)}, u32[]{:S(2)}) collective-permute-start(f32[2,1,1]{0,2,1:T(1,128)S(1)} %pad_maximum_fusion.8), channel_id=1, source_target_pairs={{6,0},{7,1},{0,2},{1,3},{2,4},{3,5},{4,6},{5,7},{14,8},{15,9},{8,1... | collective-permute-start | bytes 32 | tf_op jit(solution)/shard_map/ppermute | solution.py:216
  358.1 6.6 %collective-permute-start.12 = (f32[2,1,1]{0,2,1:T(1,128)S(1)}, f32[2,1,1]{0,2,1:T(1,128)S(1)}, u32[]{:S(2)}, u32[]{:S(2)}) collective-permute-start(f32[2,1,1]{0,2,1:T(1,128)S(1)} %pad_maximum_fusion.8), channel_id=1, source_target_pairs={{5,0},{6,1},{7,2},{0,3},{1,4},{2,5},{3,6},{4,7},{13,8},{14,9},{15,... | collective-permute-start | bytes 32 | tf_op jit(solution)/shard_map/ppermute | solution.py:216
  360.3 4.4 %collective-permute-start.13 = (f32[2,1,1]{0,2,1:T(1,128)S(1)}, f32[2,1,1]{0,2,1:T(1,128)S(1)}, u32[]{:S(2)}, u32[]{:S(2)}) collective-permute-start(f32[2,1,1]{0,2,1:T(1,128)S(1)} %pad_maximum_fusion.8), channel_id=1, source_target_pairs={{4,0},{5,1},{6,2},{7,3},{0,4},{1,5},{2,6},{3,7},{12,8},{13,9},{14,... | collective-permute-start | bytes 32 | tf_op jit(solution)/shard_map/ppermute | solution.py:216
  360.8 3.8 collective-permute-start.14
  361.0 3.7 collective-permute-start.15
  362.5 3.5 collective-permute-start.16
  366.1 14.2 %collective-permute-start.17 = (f32[2,1,1]{0,2,1:T(1,128)S(1)}, f32[2,1,1]{0,2,1:T(1,128)S(1)}, u32[]{:S(2)}, u32[]{:S(2)}) collective-permute-start(f32[2,1,1]{0,2,1:T(1,128)S(1)} %fusion.120), channel_id=1, source_target_pairs={{24,0},{25,1},{26,2},{27,3},{28,4},{29,5},{30,6},{31,7},{0,8},{1,9... | collective-permute-start | bytes 32 | tf_op jit(solution)/shard_map/ppermute | solution.py:216
  367.6 21.8 %collective-permute-start.18 = (f32[2,1,1]{0,2,1:T(1,128)S(1)}, f32[2,1,1]{0,2,1:T(1,128)S(1)}, u32[]{:S(2)}, u32[]{:S(2)}) collective-permute-start(f32[2,1,1]{0,2,1:T(1,128)S(1)} %fusion.120), channel_id=1, source_target_pairs={{16,0},{17,1},{18,2},{19,3},{20,4},{21,5},{22,6},{23,7},{24,8},{25... | collective-permute-start | bytes 32 | tf_op jit(solution)/shard_map/ppermute | solution.py:216
  370.0 19.4 %collective-permute-start.19 = (f32[2,1,1]{0,2,1:T(1,128)S(1)}, f32[2,1,1]{0,2,1:T(1,128)S(1)}, u32[]{:S(2)}, u32[]{:S(2)}) collective-permute-start(f32[2,1,1]{0,2,1:T(1,128)S(1)} %fusion.120), channel_id=1, source_target_pairs={{8,0},{9,1},{10,2},{11,3},{12,4},{13,5},{14,6},{15,7},{16,8},{17,9... | collective-permute-start | bytes 32 | tf_op jit(solution)/shard_map/ppermute | solution.py:216
  408.7 2.1 copy-start.6
  411.4 0.8 copy-start.13
